TPU v7x, 256 devices: a whole 4x4x8 slice. The times are simulated.
256 devices in a mesh: section: 16 (over z_lo, x, core), tp: 16 (over y, z_hi).
Axes of the slice: x: 4, y: 4, z: 8 (z_hi: 4, z_lo: 2; z = z_hi * 2 + z_lo), core: 2. Of those that a mesh axis runs over, the one named last changes fastest.
Arguments:
- tokens: bfloat16 [2, 512, 4096], P(None, 'tp'), may hold values from -6 to 6
- norm_gains: float32 [2, 4096], replicated, may hold values from 0.1 to 1.9
- w_gate: bfloat16 [16, 4096, 2048], P('section', None, 'tp'), may hold values from -0.09375 to 0.09375
- w_up: bfloat16 [16, 4096, 2048], P('section', None, 'tp'), may hold values from -0.09375 to 0.09375
- w_down: bfloat16 [16, 2048, 4096], P('section', 'tp'), may hold values from -0.0625 to 0.0625
Outputs:
- acts: bfloat16 [16, 2, 512, 512], P('section', None, 'tp')
All inputs are finite; a program needn't handle non-finite values.
Results may differ from a plain program's by a relative error of at most 0.022.
Values may be sent and summed in bfloat16 or wider, within the bound.
No kernel may reach another device: no remote copies, remote signals or barrier semaphores. Data moves between devices by JAX's collectives and lax.ppermute only.
A program may use at most 64 MiB of HBM per device.

v0:
```python
import jax
import jax.numpy as jnp
from jax import lax
from jax.sharding import PartitionSpec as P

LAYERS = 2
PIECES = 1
epsilon = 1e-05


def swapped(value, axis, mask):
    pairs = [(source, source ^ mask) for source in range(lax.axis_size(axis))]
    return lax.ppermute(value, axis, pairs)


def shifted(value, axis, steps):
    count = lax.axis_size(axis)
    return lax.ppermute(value, axis, [(source, source + steps) for source in range(count - steps)])


def body(tokens, norm_gains, w_gate, w_up, w_down):
    section_count = lax.axis_size("section")
    split = section_count // LAYERS
    bit_count = split.bit_length() - 1
    position = lax.axis_index("section")
    section_layer = position // split
    member = position % split
    core = member % 2
    xpos = member // 2
    x_count = split // 2
    micro_count, tok_dev, model_width = tokens.shape
    piece_width = model_width // split
    half_width = model_width // 2
    row_count = tok_dev // PIECES
    piece_count = micro_count * PIECES
    tick_count = piece_count + LAYERS - 1

    def pick(value, axis, which):
        shape = value.shape
        grouped = value.reshape(shape[:axis] + (x_count, 2, piece_width) + shape[axis + 1 :])
        chosen = lax.dynamic_index_in_dim(grouped, which, axis + 1, keepdims=False)
        return chosen.reshape(shape[:axis] + (half_width,) + shape[axis + 1 :])

    other = 1 - core
    gate_own = pick(w_gate[0], 0, core)
    gate_other = pick(w_gate[0], 0, other)
    up_own = pick(w_up[0], 0, core)
    up_other = pick(w_up[0], 0, other)
    down_own = pick(w_down[0], 1, core)
    down_other = pick(w_down[0], 1, other)
    norm_gain = lax.dynamic_index_in_dim(norm_gains, section_layer, 0, keepdims=False)
    gain_own = pick(norm_gain, 0, core)

    def from_tokens(piece_index):
        micro_index, part = divmod(piece_index, PIECES)
        rows = tokens[micro_index, part * row_count : (part + 1) * row_count].astype(jnp.float32)
        return (pick(rows, 1, core), jnp.sum(rows * rows, axis=1, keepdims=True))

    def from_received(received):
        current = received.astype(jnp.float32)
        own_sq = jnp.sum(current * current, axis=1, keepdims=True)
        return (current, own_sq + swapped(own_sq, "section", 1))

    def tick(current, square_sum):
        inv_rms = lax.rsqrt(square_sum / model_width + epsilon)
        normed = (current * inv_rms * gain_own).astype(jnp.bfloat16)
        gathered = lax.all_gather(normed, "tp", axis=0, tiled=True)
        gathered_other = swapped(gathered, "section", 1)
        gate_proj = jnp.dot(gathered, gate_own, preferred_element_type=jnp.float32) + jnp.dot(
            gathered_other, gate_other, preferred_element_type=jnp.float32
        )
        up_proj = jnp.dot(gathered, up_own, preferred_element_type=jnp.float32) + jnp.dot(
            gathered_other, up_other, preferred_element_type=jnp.float32
        )
        active = (jax.nn.silu(gate_proj) * up_proj).astype(jnp.bfloat16)
        part_other = jnp.dot(active, down_other, preferred_element_type=jnp.float32).astype(
            jnp.bfloat16
        )
        part_from_other = swapped(part_other, "section", 1)
        part_own = jnp.dot(active, down_own, preferred_element_type=jnp.float32).astype(
            jnp.bfloat16
        )
        pair = (part_own.astype(jnp.float32) + part_from_other.astype(jnp.float32)).astype(
            jnp.bfloat16
        )
        summed = lax.psum_scatter(pair, "tp", scatter_dimension=0, tiled=True)
        for level in range(1, bit_count):
            summed = summed.astype(jnp.float32) + swapped(summed, "section", 1 << level).astype(
                jnp.float32
            )
            if level < bit_count - 1:
                summed = summed.astype(jnp.bfloat16)
        full_half = (current + summed.astype(jnp.float32)).astype(jnp.bfloat16)
        block = lax.dynamic_index_in_dim(
            full_half.reshape(row_count, x_count, piece_width), xpos, 1, keepdims=False
        )
        return (full_half, block)

    blocks = []
    received = None
    for tick_index in range(tick_count):
        if tick_index == 0:
            current, square_sum = from_tokens(0)
        elif tick_index >= piece_count:
            current, square_sum = from_received(received)
        else:
            first_current, first_sum = from_tokens(tick_index)
            later_current, later_sum = from_received(received)
            is_first = section_layer == 0
            current = jnp.where(is_first, first_current, later_current)
            square_sum = jnp.where(is_first, first_sum, later_sum)
        full_half, block = tick(current, square_sum)
        blocks.append(block)
        if tick_index < tick_count - 1:
            received = shifted(full_half, "section", split)
    stacked = jnp.stack(blocks, axis=0)
    outputs = []
    for micro_index in range(micro_count):
        parts = [
            lax.dynamic_index_in_dim(
                stacked, micro_index * PIECES + part + section_layer, 0, keepdims=False
            )
            for part in range(PIECES)
        ]
        outputs.append(jnp.concatenate(parts, axis=0))
    return jnp.stack(outputs, axis=0)[None]


def solution(mesh):
    in_specs = (
        P(None, "tp", None),
        P(),
        P("section", None, "tp"),
        P("section", None, "tp"),
        P("section", "tp", None),
    )
    out_specs = P("section", None, "tp", None)
    return jax.shard_map(body, mesh=mesh, in_specs=in_specs, out_specs=out_specs, check_vma=False)
```

profile of v0, /device:TPU:6, one launch (start us, length us, event | category | flops | bytes accessed | tf_op | source)
XLA Modules:
  0.0 558.7 jit_solution(12921306199294246905)
XLA Ops:
  12.4 62.2 %all-gather.4.cloned.1.call-done = bf16[512,2048]{1,0:T(8,128)(2,1)} async-done(((bf16[32,2048]{1,0:T(8,128)(2,1)}), bf16[512,2048]{1,0:T(8,128)(2,1)}) %all-gather.4.cloned.1.call-update) | async-done | bytes 2097168 | tf_op jit(solution)/shard_map/all_gather | solution.py:67
  80.0 2.3 convolution_add_fusion.5
  82.3 2.3 fusion.3
  85.9 3.8 collective-permute-done.1
  89.7 2.1 add_convert_fusion.2
  91.9 88.2 %reduce-scatter.4.cloned.1.call-done = bf16[32,2048]{1,0:T(8,128)(2,1)} async-done(((bf16[512,2048]{1,0:T(8,128)(2,1)}), bf16[32,2048]{1,0:T(8,128)(2,1)}) %reduce-scatter.4.cloned.1.call-update) | async-done | bytes 131088 | tf_op jit(solution)/shard_map/reduce_scatter | solution.py:86
  180.8 4.9 collective-permute-done.2
  187.6 5.6 %collective-permute-done.3 = bf16[32,2048]{1,0:T(8,128)(2,1)S(1)} collective-permute-done((bf16[32,2048]{1,0:T(8,128)(2,1)S(1)}, bf16[32,2048]{1,0:T(8,128)(2,1)S(1)}, u32[]{:S(2)}, u32[]{:S(2)}) %collective-permute-start.3) | collective-permute-done | bytes 131104 | tf_op jit(solution)/shard_map/ppermute | solution.py:13
  194.9 2.5 collective-permute-done.4
  199.6 58.4 %all-gather.6.cloned.1.call-done = bf16[512,2048]{1,0:T(8,128)(2,1)} async-done(((bf16[32,2048]{1,0:T(8,128)(2,1)}), bf16[512,2048]{1,0:T(8,128)(2,1)}) %all-gather.6.cloned.1.call-update) | async-done | bytes 2097168 | tf_op jit(solution)/shard_map/all_gather | solution.py:67
  258.0 2.4 fusion.15
  264.7 4.0 collective-permute-done.7
  268.7 2.1 add_convert_fusion.1
  270.9 88.1 %reduce-scatter.6.cloned.1.call-done = bf16[32,2048]{1,0:T(8,128)(2,1)} async-done(((bf16[512,2048]{1,0:T(8,128)(2,1)}), bf16[32,2048]{1,0:T(8,128)(2,1)}) %reduce-scatter.6.cloned.1.call-update) | async-done | bytes 131088 | tf_op jit(solution)/shard_map/reduce_scatter | solution.py:86
  359.8 4.8 collective-permute-done.8
  366.6 5.5 collective-permute-done.9
  373.8 2.5 collective-permute-done.10
  378.5 58.4 %all-gather.8.cloned.1.call-done = bf16[512,2048]{1,0:T(8,128)(2,1)} async-done(((bf16[32,2048]{1,0:T(8,128)(2,1)}), bf16[512,2048]{1,0:T(8,128)(2,1)}) %all-gather.8.cloned.1.call-update) | async-done | bytes 2097168 | tf_op jit(solution)/shard_map/all_gather | solution.py:67
  436.9 2.5 fusion.17
  443.7 4.0 collective-permute-done.13
  447.7 2.1 add_convert_fusion
  449.8 88.1 %reduce-scatter.8.cloned.1.call-done = bf16[32,2048]{1,0:T(8,128)(2,1)} async-done(((bf16[512,2048]{1,0:T(8,128)(2,1)}), bf16[32,2048]{1,0:T(8,128)(2,1)}) %reduce-scatter.8.cloned.1.call-update) | async-done | bytes 131088 | tf_op jit(solution)/shard_map/reduce_scatter | solution.py:86
  538.8 4.7 collective-permute-done.14
  545.8 5.2 collective-permute-done.15
  (97 shorter events, 38.5 us)
Async XLA Ops:
  6.5 4.9 copy-start
  6.5 68.1 %all-gather.4.cloned.1.call-start = ((), (), s32[]{:S(2)}) async-start(), calls=%async_computation.3 | async-start | bytes 2228224 | tf_op jit(solution)/shard_map/all_gather | solution.py:67
  12.4 167.7 %reduce-scatter.4.cloned.1.call-start = ((), (), s32[]{:S(2)}) async-start(), calls=%async_computation.4 | async-start | bytes 2228224 | tf_op jit(solution)/shard_map/reduce_scatter | solution.py:86
  74.6 5.4 collective-permute-start
  78.2 4.1 copy-start.4
  85.3 4.4 collective-permute-start.1
  91.8 166.2 %all-gather.6.cloned.1.call-start = ((), (), s32[]{:S(2)}) async-start(), calls=%async_computation.5 | async-start | bytes 2228224 | tf_op jit(solution)/shard_map/all_gather | solution.py:67
  180.0 5.7 %collective-permute-start.2 = (bf16[32,2048]{1,0:T(8,128)(2,1)}, bf16[32,2048]{1,0:T(8,128)(2,1)S(1)}, u32[]{:S(2)}, u32[]{:S(2)}) collective-permute-start(bf16[32,2048]{1,0:T(8,128)(2,1)} %reduce-scatter.4.cloned.1.call-done), channel_id=1, source_target_pairs={{0,32},{16,48},{32,0},{48,16},{64,96},{80,112},{96,64},{112,80},{1... | collective-permute-start | bytes 393224 | tf_op jit(solution)/shard_map/ppermute | solution.py:13
  186.7 6.6 %collective-permute-start.3 = (bf16[32,2048]{1,0:T(8,128)(2,1)S(1)}, bf16[32,2048]{1,0:T(8,128)(2,1)S(1)}, u32[]{:S(2)}, u32[]{:S(2)}) collective-permute-start(bf16[32,2048]{1,0:T(8,128)(2,1)S(1)} %add_convert_fusion.7), channel_id=1, source_target_pairs={{0,64},{16,80},{32,96},{48,112},{64,0},{80,16},{96,32},{112,48},{1... | collective-permute-start | bytes 393224 | tf_op jit(solution)/shard_map/ppermute | solution.py:13
  193.3 4.1 collective-permute-start.4
  197.5 1.2 collective-permute-start.5
  199.5 159.4 %reduce-scatter.6.cloned.1.call-start = ((), (), s32[]{:S(2)}) async-start(), calls=%async_computation.6 | async-start | bytes 2228224 | tf_op jit(solution)/shard_map/reduce_scatter | solution.py:86
  258.0 4.4 collective-permute-start.6
  264.5 4.2 collective-permute-start.7
  270.8 166.1 %all-gather.8.cloned.1.call-start = ((), (), s32[]{:S(2)}) async-start(), calls=%async_computation.7 | async-start | bytes 2228224 | tf_op jit(solution)/shard_map/all_gather | solution.py:67
  358.9 5.6 %collective-permute-start.8 = (bf16[32,2048]{1,0:T(8,128)(2,1)}, bf16[32,2048]{1,0:T(8,128)(2,1)S(1)}, u32[]{:S(2)}, u32[]{:S(2)}) collective-permute-start(bf16[32,2048]{1,0:T(8,128)(2,1)} %reduce-scatter.6.cloned.1.call-done), channel_id=1, source_target_pairs={{0,32},{16,48},{32,0},{48,16},{64,96},{80,112},{96,64},{112,80},{1... | collective-permute-start | bytes 393224 | tf_op jit(solution)/shard_map/ppermute | solution.py:13
  365.5 6.6 %collective-permute-start.9 = (bf16[32,2048]{1,0:T(8,128)(2,1)S(1)}, bf16[32,2048]{1,0:T(8,128)(2,1)S(1)}, u32[]{:S(2)}, u32[]{:S(2)}) collective-permute-start(bf16[32,2048]{1,0:T(8,128)(2,1)S(1)} %add_convert_fusion.5), channel_id=1, source_target_pairs={{0,64},{16,80},{32,96},{48,112},{64,0},{80,16},{96,32},{112,48},{1... | collective-permute-start | bytes 393224 | tf_op jit(solution)/shard_map/ppermute | solution.py:13
  372.1 4.2 collective-permute-start.10
  376.5 1.2 collective-permute-start.11
  378.5 159.3 %reduce-scatter.8.cloned.1.call-start = ((), (), s32[]{:S(2)}) async-start(), calls=%async_computation.8 | async-start | bytes 2228224 | tf_op jit(solution)/shard_map/reduce_scatter | solution.py:86
  436.9 4.4 collective-permute-start.12
  443.5 4.2 collective-permute-start.13
  537.8 5.6 %collective-permute-start.14 = (bf16[32,2048]{1,0:T(8,128)(2,1)}, bf16[32,2048]{1,0:T(8,128)(2,1)S(1)}, u32[]{:S(2)}, u32[]{:S(2)}) collective-permute-start(bf16[32,2048]{1,0:T(8,128)(2,1)} %reduce-scatter.8.cloned.1.call-done), channel_id=1, source_target_pairs={{0,32},{16,48},{32,0},{48,16},{64,96},{80,112},{96,64},{112,80},{1... | collective-permute-start | bytes 393224 | tf_op jit(solution)/shard_map/ppermute | solution.py:13
  544.4 6.6 %collective-permute-start.15 = (bf16[32,2048]{1,0:T(8,128)(2,1)S(1)}, bf16[32,2048]{1,0:T(8,128)(2,1)S(1)}, u32[]{:S(2)}, u32[]{:S(2)}) collective-permute-start(bf16[32,2048]{1,0:T(8,128)(2,1)S(1)} %add_convert_fusion.3), channel_id=1, source_target_pairs={{0,64},{16,80},{32,96},{48,112},{64,0},{80,16},{96,32},{112,48},{1... | collective-permute-start | bytes 393224 | tf_op jit(solution)/shard_map/ppermute | solution.py:13
  (5 other events, 11.0 us)
Sparse Core Ops, SparseCore 0:
  12.5 62.0 all-gather.3
  91.9 88.0 reduce-scatter.3
  199.6 58.2 all-gather.5
  270.9 87.9 reduce-scatter.5
  378.6 58.2 all-gather.7
  449.9 87.8 reduce-scatter.7
where the time goes:
time: 559 us
  waiting for transfers between devices  495 us (89%)
  matrix products  23.5 us (4%)
  between operations  13.9 us (2%)
  starting transfers between devices  10.3 us (2%)
  other arithmetic  8.52 us (2%)
  local copies, waits for them, and re-layouts  7.12 us (1%)
    reduce_scatter x3, waiting for transfers between devices, tick(): summed = lax.psum_scatter(pair, 'tp', scatter_dimension=0, tiled=True)  264 us
    all_gather x3, waiting for transfers between devices, tick(): gathered = lax.all_gather(normed, 'tp', axis=0, tiled=True)  179 us
    ppermute x14, waiting for transfers between devices, swapped(): return lax.ppermute(value, axis, pairs)  47 us
  transfers between devices with their start and end apart: 22, of which 21 were waited for; matrix products, arithmetic and copies ran while one was open for 2% of the time, Pallas kernels for 0%

commit v1 on v0

--- a/solution.py
+++ b/solution.py
@@ -64,7 +64,9 @@
     def tick(current, square_sum):
         inv_rms = lax.rsqrt(square_sum / model_width + epsilon)
         normed = (current * inv_rms * gain_own).astype(jnp.bfloat16)
-        gathered = lax.all_gather(normed, "tp", axis=0, tiled=True)
+        gathered = jnp.concatenate(
+            lax.all_to_all(jnp.stack([normed] * lax.axis_size("tp")), "tp", 0, 0), axis=0
+        )
         gathered_other = swapped(gathered, "section", 1)
         gate_proj = jnp.dot(gathered, gate_own, preferred_element_type=jnp.float32) + jnp.dot(
             gathered_other, gate_other, preferred_element_type=jnp.float32

time: 559 us -> 554 us (level)
  waiting for transfers between devices: 495 us -> 333 us
  blocking collectives: 0 us -> 159 us
    all_gather x3 -> x0, waiting for transfers between devices: 179 us -> none  [tick(): gathered = lax.all_gather(normed, 'tp', axis=0, tiled=True)]
    all_to_all x0 -> x3, blocking collectives: none -> 159 us  [tick(): lax.all_to_all(jnp.stack([normed] * lax.axis_size('tp')), 'tp', 0, 0)]
    reduce_scatter x3, waiting for transfers between devices: 264 us -> 279 us  [tick(): summed = lax.psum_scatter(pair, 'tp', scatter_dimension=0, tiled=True)]
  transfers between devices with their start and end apart: 22 -> 19, of which waited for: 21 -> 18; matrix products, arithmetic and copies ran while one was open for 2% -> 2% of each run, Pallas kernels for 0% -> 0%
where the time goes in v1:
time: 554 us; the launch traced here: 553 us
  waiting for transfers between devices  333 us (60%)
  blocking collectives  159 us (29%)
  matrix products  20 us (4%)
  between operations  13.6 us (2%)
  local copies, waits for them, and re-layouts  10.3 us (2%)
  starting transfers between devices  10.3 us (2%)
  other arithmetic  6.56 us (1%)
    reduce_scatter x3, waiting for transfers between devices, tick(): summed = lax.psum_scatter(pair, 'tp', scatter_dimension=0, tiled=True)  279 us
    all_to_all x3, blocking collectives, tick(): lax.all_to_all(jnp.stack([normed] * lax.axis_size('tp')), 'tp', 0, 0)  159 us
    ppermute x14, waiting for transfers between devices, swapped(): return lax.ppermute(value, axis, pairs)  49.4 us
  transfers between devices with their start and end apart: 19, of which 18 were waited for; matrix products, arithmetic and copies ran while one was open for 2% of the time, Pallas kernels for 0%

profile of v1, /device:TPU:6, one launch (start us, length us, event | category | flops | bytes accessed | tf_op | source)
XLA Modules:
  0.0 553.2 jit_solution(9434007852240045671)
XLA Ops:
  9.8 2.2 dynamic-slice_reduce_fusion
  12.6 61.2 %all_to_all.15 = bf16[16,32,2048]{2,1,0:T(8,128)(2,1)S(1)} all-to-all(bf16[16,32,2048]{2,1,0:T(8,128)(2,1)S(1)} %stack.16), channel_id=1, replica_groups=mesh['section'=16,'tp'=16] {'tp'}, dimensions={0} | all-to-all | bytes 4194304 | tf_op jit(solution)/shard_map/all_to_all | solution.py:68
  79.8 2.3 convolution_add_fusion.5
  82.1 2.3 fusion.3
  85.8 3.8 collective-permute-done.1
  89.5 2.1 add_convert_fusion.2
  91.7 87.7 %reduce-scatter.4.cloned.1.call-done = bf16[32,2048]{1,0:T(8,128)(2,1)} async-done(((bf16[512,2048]{1,0:T(8,128)(2,1)}), bf16[32,2048]{1,0:T(8,128)(2,1)}) %reduce-scatter.4.cloned.1.call-update) | async-done | bytes 131088 | tf_op jit(solution)/shard_map/reduce_scatter | solution.py:88
  180.2 4.9 collective-permute-done.2
  187.0 5.5 %collective-permute-done.3 = bf16[32,2048]{1,0:T(8,128)(2,1)S(1)} collective-permute-done((bf16[32,2048]{1,0:T(8,128)(2,1)S(1)}, bf16[32,2048]{1,0:T(8,128)(2,1)S(1)}, u32[]{:S(2)}, u32[]{:S(2)}) %collective-permute-start.3) | collective-permute-done | bytes 131104 | tf_op jit(solution)/shard_map/ppermute | solution.py:13
  194.2 2.5 collective-permute-done.4
  198.4 49.0 %all_to_all.16 = bf16[16,32,2048]{2,1,0:T(8,128)(2,1)S(1)} all-to-all(bf16[16,32,2048]{2,1,0:T(8,128)(2,1)S(1)} %stack.18), channel_id=1, replica_groups=mesh['section'=16,'tp'=16] {'tp'}, dimensions={0} | all-to-all | bytes 4194304 | tf_op jit(solution)/shard_map/all_to_all | solution.py:68
  249.2 2.4 collective-permute-done.6
  254.3 4.0 collective-permute-done.7
  258.3 2.1 add_convert_fusion.1
  260.5 95.5 %reduce-scatter.6.cloned.1.call-done = bf16[32,2048]{1,0:T(8,128)(2,1)} async-done(((bf16[512,2048]{1,0:T(8,128)(2,1)}), bf16[32,2048]{1,0:T(8,128)(2,1)}) %reduce-scatter.6.cloned.1.call-update) | async-done | bytes 131088 | tf_op jit(solution)/shard_map/reduce_scatter | solution.py:88
  356.8 4.8 collective-permute-done.8
  363.7 5.5 collective-permute-done.9
  370.9 2.5 collective-permute-done.10
  375.1 49.0 %all_to_all.17 = bf16[16,32,2048]{2,1,0:T(8,128)(2,1)S(1)} all-to-all(bf16[16,32,2048]{2,1,0:T(8,128)(2,1)S(1)} %stack.20), channel_id=1, replica_groups=mesh['section'=16,'tp'=16] {'tp'}, dimensions={0} | all-to-all | bytes 4194304 | tf_op jit(solution)/shard_map/all_to_all | solution.py:68
  425.9 2.4 collective-permute-done.12
  431.0 4.0 collective-permute-done.13
  437.1 95.5 %reduce-scatter.8.cloned.1.call-done = bf16[32,2048]{1,0:T(8,128)(2,1)} async-done(((bf16[512,2048]{1,0:T(8,128)(2,1)}), bf16[32,2048]{1,0:T(8,128)(2,1)}) %reduce-scatter.8.cloned.1.call-update) | async-done | bytes 131088 | tf_op jit(solution)/shard_map/reduce_scatter | solution.py:88
  533.5 4.7 collective-permute-done.14
  540.5 5.2 collective-permute-done.15
  (108 shorter events, 38.5 us)
Async XLA Ops:
  6.5 172.8 %reduce-scatter.4.cloned.1.call-start = ((), (), s32[]{:S(2)}) async-start(), calls=%async_computation.6 | async-start | bytes 2228224 | tf_op jit(solution)/shard_map/reduce_scatter | solution.py:88
  12.6 61.3 %copy-start.10 = (bf16[1,128,4096]{2,1,0:T(8,128)(2,1)S(1)}, bf16[1,128,4096]{2,1,0:T(8,128)(2,1)}, u32[]{:S(2)}) copy-start(bf16[1,128,4096]{2,1,0:T(8,128)(2,1)} %param.9) | copy-start | bytes 3145732
  73.8 6.0 %collective-permute-start = (bf16[512,2048]{1,0:T(8,128)(2,1)S(1)}, bf16[512,2048]{1,0:T(8,128)(2,1)}, u32[]{:S(2)}, u32[]{:S(2)}) collective-permute-start(bf16[512,2048]{1,0:T(8,128)(2,1)S(1)} %bitcast.76), channel_id=1, source_target_pairs={{0,16},{16,0},{32,48},{48,32},{64,80},{80,64},{96,112},{112,96},{1... | collective-permute-start | bytes 6291464 | tf_op jit(solution)/shard_map/ppermute | solution.py:13
  76.4 8.0 %copy-start.7 = (bf16[128,4,1,512]{0,3,2,1:T(8,128)(2,1)}, bf16[128,4,1,512]{0,3,2,1:T(8,128)(2,1)S(1)}, u32[]{:S(2)}) copy-start(bf16[128,4,1,512]{0,3,2,1:T(8,128)(2,1)S(1)} %get-tuple-element.8) | copy-start | bytes 1572868
  85.2 4.4 collective-permute-start.1
  91.6 105.3 %copy-start.11 = (f32[32,4,512]{2,1,0:T(4,128)S(1)}, f32[32,4,512]{2,1,0:T(4,128)}, u32[]{:S(2)}) copy-start(f32[32,4,512]{2,1,0:T(4,128)} %get-tuple-element.17) | copy-start | bytes 786436
  91.6 264.4 %reduce-scatter.6.cloned.1.call-start = ((), (), s32[]{:S(2)}) async-start(), calls=%async_computation.7 | async-start | bytes 2228224 | tf_op jit(solution)/shard_map/reduce_scatter | solution.py:88
  179.4 5.7 %collective-permute-start.2 = (bf16[32,2048]{1,0:T(8,128)(2,1)}, bf16[32,2048]{1,0:T(8,128)(2,1)S(1)}, u32[]{:S(2)}, u32[]{:S(2)}) collective-permute-start(bf16[32,2048]{1,0:T(8,128)(2,1)} %reduce-scatter.4.cloned.1.call-done), channel_id=1, source_target_pairs={{0,32},{16,48},{32,0},{48,16},{64,96},{80,112},{96,64},{112,80},{1... | collective-permute-start | bytes 393224 | tf_op jit(solution)/shard_map/ppermute | solution.py:13
  186.0 6.6 %collective-permute-start.3 = (bf16[32,2048]{1,0:T(8,128)(2,1)S(1)}, bf16[32,2048]{1,0:T(8,128)(2,1)S(1)}, u32[]{:S(2)}, u32[]{:S(2)}) collective-permute-start(bf16[32,2048]{1,0:T(8,128)(2,1)S(1)} %add_convert_fusion.7), channel_id=1, source_target_pairs={{0,64},{16,80},{32,96},{48,112},{64,0},{80,16},{96,32},{112,48},{1... | collective-permute-start | bytes 393224 | tf_op jit(solution)/shard_map/ppermute | solution.py:13
  192.6 4.1 collective-permute-start.4
  196.8 1.2 collective-permute-start.5
  198.4 49.0 %copy-start.5 = (bf16[4,1,512,128]{3,2,1,0:T(8,128)(2,1)S(1)}, bf16[4,1,512,128]{3,2,1,0:T(8,128)(2,1)}, u32[]{:S(2)}) copy-start(bf16[4,1,512,128]{3,2,1,0:T(8,128)(2,1)} %copy-done.4) | copy-start | bytes 1572868
  247.4 4.2 collective-permute-start.6
  254.1 4.2 collective-permute-start.7
  260.4 272.2 %reduce-scatter.8.cloned.1.call-start = ((), (), s32[]{:S(2)}) async-start(), calls=%async_computation.8 | async-start | bytes 2228224 | tf_op jit(solution)/shard_map/reduce_scatter | solution.py:88
  356.0 5.6 %collective-permute-start.8 = (bf16[32,2048]{1,0:T(8,128)(2,1)}, bf16[32,2048]{1,0:T(8,128)(2,1)S(1)}, u32[]{:S(2)}, u32[]{:S(2)}) collective-permute-start(bf16[32,2048]{1,0:T(8,128)(2,1)} %reduce-scatter.6.cloned.1.call-done), channel_id=1, source_target_pairs={{0,32},{16,48},{32,0},{48,16},{64,96},{80,112},{96,64},{112,80},{1... | collective-permute-start | bytes 393224 | tf_op jit(solution)/shard_map/ppermute | solution.py:13
  362.6 6.6 %collective-permute-start.9 = (bf16[32,2048]{1,0:T(8,128)(2,1)S(1)}, bf16[32,2048]{1,0:T(8,128)(2,1)S(1)}, u32[]{:S(2)}, u32[]{:S(2)}) collective-permute-start(bf16[32,2048]{1,0:T(8,128)(2,1)S(1)} %add_convert_fusion.5), channel_id=1, source_target_pairs={{0,64},{16,80},{32,96},{48,112},{64,0},{80,16},{96,32},{112,48},{1... | collective-permute-start | bytes 393224 | tf_op jit(solution)/shard_map/ppermute | solution.py:13
  369.2 4.2 collective-permute-start.10
  373.5 1.2 collective-permute-start.11
  375.1 49.1 %copy-start.6 = (bf16[4,1,512,128]{3,2,1,0:T(8,128)(2,1)S(1)}, bf16[4,1,512,128]{3,2,1,0:T(8,128)(2,1)}, u32[]{:S(2)}) copy-start(bf16[4,1,512,128]{3,2,1,0:T(8,128)(2,1)} %copy-done.4) | copy-start | bytes 1572868
  424.2 4.2 collective-permute-start.12
  430.8 4.2 collective-permute-start.13
  532.6 5.6 %collective-permute-start.14 = (bf16[32,2048]{1,0:T(8,128)(2,1)}, bf16[32,2048]{1,0:T(8,128)(2,1)S(1)}, u32[]{:S(2)}, u32[]{:S(2)}) collective-permute-start(bf16[32,2048]{1,0:T(8,128)(2,1)} %reduce-scatter.8.cloned.1.call-done), channel_id=1, source_target_pairs={{0,32},{16,48},{32,0},{48,16},{64,96},{80,112},{96,64},{112,80},{1... | collective-permute-start | bytes 393224 | tf_op jit(solution)/shard_map/ppermute | solution.py:13
  539.2 6.6 %collective-permute-start.15 = (bf16[32,2048]{1,0:T(8,128)(2,1)S(1)}, bf16[32,2048]{1,0:T(8,128)(2,1)S(1)}, u32[]{:S(2)}, u32[]{:S(2)}) collective-permute-start(bf16[32,2048]{1,0:T(8,128)(2,1)S(1)} %add_convert_fusion.3), channel_id=1, source_target_pairs={{0,64},{16,80},{32,96},{48,112},{64,0},{80,16},{96,32},{112,48},{1... | collective-permute-start | bytes 393224 | tf_op jit(solution)/shard_map/ppermute | solution.py:13
  (9 other events, 19.6 us)
Sparse Core Ops, SparseCore 0:
  91.8 87.5 reduce-scatter.3
  260.5 95.3 reduce-scatter.5
  437.2 95.3 reduce-scatter.7
